TPU v7x, 512 devices: a whole 4x4x16 slice. The times are simulated.
512 devices in a mesh: seq: 32 (over z_lo, y), tensor: 8 (over z_hi, x), enc: 2 (over core).
Axes of the slice: x: 4, y: 4, z: 16 (z_hi: 2, z_lo: 8; z = z_hi * 8 + z_lo), core: 2. Of those that a mesh axis runs over, the one named last changes fastest.
Arguments:
- neighbour_rows: bfloat16 [32768, 1024], P('seq'), may hold values from -17 to 17
- norm_gain: float32 [1024], replicated, may hold values from 0.1 to 1.9
- up_weight: bfloat16 [1024, 4096], P(None, ('tensor', 'enc')), may hold values from -0.1875 to 0.1875
- down_weight: bfloat16 [4096, 1024], P(('tensor', 'enc')), may hold values from -0.09375 to 0.09375
- final_gain: float32 [1024], replicated, may hold values from 0.1 to 1.9
- key_weight: bfloat16 [1024, 4096], P(None, ('tensor', 'enc')), may hold values from -0.1875 to 0.1875
- value_weight: bfloat16 [1024, 4096], P(None, ('tensor', 'enc')), may hold values from -0.1875 to 0.1875
- queries: bfloat16 [32768, 4096], P('seq', ('tensor', 'enc')), may hold values from -170 to 170
- block_lists: int32 [512, 2], P('seq'), may hold values from 0 to 255, as said below
- live_counts: int32 [512], P('seq'), may hold values from 1 to 2
Outputs:
- attended: bfloat16 [32768, 4096], P('seq', ('tensor', 'enc'))
Inputs may be any that keep to these rules, and one draw needn't show every extreme that they name: `block_lists`: block b of the pool lies on the device of index b // 8 along seq. The two entries of a span name blocks of two different devices. Among all list entries of one device's spans (those beyond a span's count included) at most 1 name blocks of any one device, and in every draw some device's entries reach 1 for some device.
All inputs are finite; a program needn't handle non-finite values.
Results may differ from a plain program's by a relative error of at most 0.019.
The roundings to bfloat16 on the way count: a program that leaves them out, or rounds other values in their place, can miss the bound.
Values may be sent and summed in bfloat16 or wider, within the bound.
No kernel may reach another device: no remote copies, remote signals or barrier semaphores. Data moves between devices by JAX's collectives and lax.ppermute only.
A program may use at most 64 MiB of HBM per device.

v0:
```python
import math
import jax
import jax.numpy as jnp
from jax import lax
from jax.sharding import PartitionSpec as P

DH = 128
NB = 128
CL = 64
KMAX = 2
TAG = 128


def rms_scale(rows, gain):
    mean_square = jnp.mean(rows * rows, axis=-1, keepdims=True)
    return rows * lax.rsqrt(mean_square + 1e-06) * gain


def need_ranks(owners):
    need_count = owners.shape[-1]
    order_index = jnp.arange(need_count)
    same_owner = owners[..., :, None] == owners[..., None, :]
    earlier = order_index[None, :] < order_index[:, None]
    return jnp.sum(jnp.logical_and(same_owner, earlier), axis=-1)


def shards(
    neighbour_rows,
    norm_gain,
    up_weight,
    down_weight,
    final_gain,
    key_weight,
    value_weight,
    queries,
    block_lists,
    live_counts,
):
    block_rows = neighbour_rows.shape[0]
    blocks = block_rows // NB
    head_width = key_weight.shape[1]
    heads_local = head_width // DH
    seq_count = lax.axis_size("seq")
    span_count = live_counts.shape[0]
    need_count = span_count * KMAX
    capacity = (need_count + seq_count - 1) // seq_count
    slots = seq_count * capacity
    q_width = CL * head_width
    flat_lists = block_lists.reshape(need_count)
    owners = flat_lists // blocks
    rank_order = need_ranks(owners)
    slot_index = owners * capacity + rank_order
    slot_range = jnp.arange(slots)
    slot_match = slot_index[None, :] == slot_range[:, None]
    entry_of_slot = jnp.sum(jnp.where(slot_match, jnp.arange(need_count)[None, :], 0), axis=1)
    filled = jnp.any(slot_match, axis=1)
    span_of_slot = entry_of_slot // KMAX
    block_of_slot = jnp.where(filled, flat_lists[entry_of_slot] % blocks, 0)
    span_queries = queries.reshape(span_count, q_width)
    sent_queries = jnp.take(span_queries, span_of_slot, axis=0)
    sent_queries = jnp.where(filled[:, None], sent_queries, jnp.zeros((), jnp.bfloat16))
    tag = jnp.broadcast_to(block_of_slot.astype(jnp.bfloat16)[:, None], (slots, TAG))
    outgoing = jnp.concatenate([sent_queries, tag], axis=1)
    incoming = lax.all_to_all(outgoing, "seq", split_axis=0, concat_axis=0, tiled=True)
    widened = neighbour_rows.astype(jnp.float32)
    normed = rms_scale(widened, norm_gain).astype(jnp.bfloat16)
    hidden = jax.nn.gelu(jnp.dot(normed, up_weight, preferred_element_type=jnp.float32)).astype(
        jnp.bfloat16
    )
    partial_sum = jnp.dot(hidden, down_weight, preferred_element_type=jnp.float32)
    reduced = lax.psum_scatter(partial_sum, ("tensor", "enc"), scatter_dimension=0, tiled=True)
    piece_rows = reduced.shape[0]
    piece = lax.axis_index("tensor") * lax.axis_size("enc") + lax.axis_index("enc")
    own_rows = lax.dynamic_slice_in_dim(neighbour_rows, piece * piece_rows, piece_rows, axis=0)
    encoded = own_rows.astype(jnp.float32) + reduced
    final_piece = rms_scale(encoded, final_gain).astype(jnp.bfloat16)
    final_rows = lax.all_gather(final_piece, ("tensor", "enc"), axis=0, tiled=True)
    key_part = jnp.dot(final_rows, key_weight, preferred_element_type=jnp.float32).astype(
        jnp.bfloat16
    )
    value_part = jnp.dot(final_rows, value_weight, preferred_element_type=jnp.float32).astype(
        jnp.bfloat16
    )
    key_blocks = key_part.reshape(blocks, NB, heads_local, DH)
    value_blocks = value_part.reshape(blocks, NB, heads_local, DH)
    in_queries = incoming[:, :q_width].reshape(slots, CL, heads_local, DH)
    in_block = incoming[:, q_width].astype(jnp.int32)
    in_block = jnp.clip(in_block, 0, blocks - 1)
    key_tiles = jnp.take(key_blocks, in_block, axis=0)
    value_tiles = jnp.take(value_blocks, in_block, axis=0)
    scores = jnp.einsum(
        "sqhd,skhd->shqk", in_queries, key_tiles, preferred_element_type=jnp.float32
    ) / math.sqrt(DH)
    local_max = jnp.max(scores, axis=-1, keepdims=True)
    weights = jnp.exp(scores - local_max)
    local_total = jnp.sum(weights, axis=-1)
    summed = jnp.einsum(
        "shqk,skhd->sqhd",
        weights.astype(jnp.bfloat16),
        value_tiles,
        preferred_element_type=jnp.float32,
    )
    stats = jnp.concatenate(
        [local_max[..., 0].reshape(slots, -1), local_total.reshape(slots, -1)], axis=1
    )
    reply = jnp.concatenate([summed.reshape(slots, q_width), stats], axis=1)
    returned = lax.all_to_all(reply, "seq", split_axis=0, concat_axis=0, tiled=True)
    stat_width = heads_local * CL
    picked = jnp.take(returned, slot_index, axis=0).reshape(span_count, KMAX, -1)
    part_sum = picked[..., :q_width].reshape(span_count, KMAX, CL, heads_local, DH)
    part_max = picked[..., q_width : q_width + stat_width].reshape(
        span_count, KMAX, heads_local, CL
    )
    part_total = picked[..., q_width + stat_width :].reshape(span_count, KMAX, heads_local, CL)
    live_mask = (jnp.arange(KMAX)[None, :] < live_counts[:, None])[:, :, None, None]
    part_max = jnp.where(live_mask, part_max, -jnp.inf)
    highest = jnp.max(part_max, axis=1, keepdims=True)
    scale = jnp.where(live_mask, jnp.exp(part_max - highest), 0.0)
    row_total = jnp.sum(scale * part_total, axis=1)
    scale_rows = jnp.transpose(scale, (0, 1, 3, 2))[..., None]
    combined = jnp.sum(jnp.where(scale_rows > 0, scale_rows * part_sum, 0.0), axis=1)
    result = combined / jnp.transpose(row_total, (0, 2, 1))[..., None]
    return result.reshape(span_count * CL, head_width).astype(jnp.bfloat16)


def solution(mesh):
    placed = (
        P("seq", None),
        P(),
        P(None, ("tensor", "enc")),
        P(("tensor", "enc"), None),
        P(),
        P(None, ("tensor", "enc")),
        P(None, ("tensor", "enc")),
        P("seq", ("tensor", "enc")),
        P("seq", None),
        P("seq"),
    )
    return jax.shard_map(
        shards, mesh=mesh, in_specs=placed, out_specs=P("seq", ("tensor", "enc")), check_vma=False
    )
```

profile of v0, /device:TPU:1, one launch (start us, length us, event | category | flops | bytes accessed | tf_op | source)
XLA Modules:
  0.0 442.7 jit_solution(8348694677223937590)
XLA Ops:
  6.5 2.2 fusion
  8.8 0.1 copy-done.2
  8.9 5.3 %fusion.33 = f32[1024,1024]{1,0:T(8,128)} fusion(bf16[256,1024]{1,0:T(8,128)(2,1)S(1)} %copy-done, bf16[1024,256]{1,0:T(8,128)(2,1)} %param.14, bf16[1024,1024]{1,0:T(8,128)(2,1)S(1)} %copy-done.2, f32[1024]{0:T(1024)S(1)} %copy-done.8, f32[1024]{0:T(1024)S(1)} %add_rsqrt_fusion), kind=kOutput, calls=%fused_computation.42 | convolution fusion | flops 1080295424 | bytes 7348224 | tf_op jit(solution)/shard_map/dot_general | solution.py:70
  14.2 0.7 copy-done.5
  15.0 0.1 reshape.338
  15.1 0.2 convert_reduce_fusion
  15.3 0.1 select_reduce_fusion
  15.4 0.7 gather_fusion.1
  16.1 0.2 reshape.340
  16.4 1.2 gather_fusion
  17.6 0.1 fusion.50
  17.7 0.2 select_select_fusion
  18.1 0.5 broadcast.391
  18.6 1.4 reduce.3
  20.0 1.6 reshape.393
  21.7 16.2 %all-to-all-start = ((bf16[32,2,8256]{2,1,0:T(2,128)(2,1)}), bf16[32,2,8256]{2,1,0:T(2,128)(2,1)}, u32[]{:S(2)}, u32[]{:S(2)}) async-start(bf16[32,2,8256]{2,1,0:T(2,128)(2,1)} %reshape.393), calls=%async_computation.1 | async-start | bytes 2129920 | tf_op jit(solution)/shard_map/all_to_all | solution.py:64
  37.9 0.2 all-gather.2.cloned.1.call-start
  38.1 145.8 %reduce-scatter.2.cloned.1.call-done = f32[64,1024]{1,0:T(8,128)} async-done(((f32[1024,1024]{1,0:T(8,128)}), f32[64,1024]{1,0:T(8,128)}) %reduce-scatter.2.cloned.1.call-update) | async-done | bytes 262160 | tf_op jit(solution)/shard_map/reduce_scatter | solution.py:71
  183.9 1.1 multiply_reduce_fusion.1
  185.0 1.7 multiply_convert_fusion
  186.8 4.4 %reshape.394 = bf16[32,1,16512]{2,1,0:T(2,128)(2,1)S(1)} reshape(bf16[32,2,8256]{2,1,0:T(2,128)(2,1)} %all-to-all-done) | data formatting | bytes 2113536
  191.2 5.3 %copy.112 = bf16[32,1,16512]{0,2,1:T(8,128)(2,1)} copy(bf16[32,1,16512]{2,1,0:T(2,128)(2,1)S(1)} %reshape.394) | data formatting | bytes 2113536 | tf_op jit(solution)/shard_map/all_to_all | solution.py:64
  196.5 3.8 slice.30
  200.3 4.9 %copy.116 = bf16[32,64,2,128]{3,1,2,0:T(8,128)(2,1)} copy(bf16[32,64,2,128]{0,3,2,1:T(8,128)(2,1)} %bitcast.63) | data formatting | bytes 2097152 | tf_op jit(solution)/shard_map/reshape | solution.py:86
  205.2 0.7 compare_and_fusion
  205.9 65.9 %all-gather.2.cloned.1.call-done = bf16[1024,1024]{1,0:T(8,128)(2,1)} async-done(((bf16[64,1024]{1,0:T(8,128)(2,1)}), bf16[1024,1024]{1,0:T(8,128)(2,1)}) %all-gather.2.cloned.1.call-update) | async-done | bytes 2097168 | tf_op jit(solution)/shard_map/all_gather | solution.py:77
  271.8 2.3 convolution_convert_fusion.1
  274.1 0.1 reshape.339
  274.2 0.1 copy.113
  274.3 0.8 copy-done.7
  275.1 2.3 convolution_convert_fusion
  277.4 0.1 reshape.342
  277.6 0.1 copy.115
  277.7 2.2 gather_fusion.4
  279.9 3.6 multiply_reduce_fusion
  283.5 0.1 reshape_squeeze_broadcast_in_dim.3
  283.6 1.3 fusion.15
  284.9 0.1 reshape.344
  285.0 2.2 gather_fusion.3
  287.2 2.4 fusion.17
  289.5 3.0 copy.117
  292.5 2.9 reshape.343
  295.5 0.1 maximum_bitcast_fusion
  295.6 3.5 copy.118
  299.1 5.3 %all-to-all-start.1 = ((f32[32,1,16640]{2,1,0:T(1,128)}), f32[32,1,16640]{2,1,0:T(1,128)}, u32[]{:S(2)}, u32[]{:S(2)}) async-start(f32[32,1,16640]{2,1,0:T(1,128)} %copy.118), calls=%async_computation.2 | async-start | bytes 4259840 | tf_op jit(solution)/shard_map/all_to_all | solution.py:107
  304.4 0.1 reshape.345
  304.8 96.1 %all-to-all-done.1 = f32[32,1,16640]{2,1,0:T(1,128)} async-done(((f32[32,1,16640]{2,1,0:T(1,128)}), f32[32,1,16640]{2,1,0:T(1,128)}, u32[]{:S(2)}, u32[]{:S(2)}) %all-to-all-start.1) | async-done | bytes 2129952 | tf_op jit(solution)/shard_map/all_to_all | solution.py:107
  400.9 1.7 copy.143
  402.7 2.5 gather_fusion.2
  405.2 3.5 gather.19
  408.7 1.8 copy_select_fusion
  410.8 0.1 reshape.346
  410.9 0.1 broadcast_compare_fusion
  411.0 0.5 copy.123
  411.5 0.2 copy.125
  411.8 4.3 broadcast_in_dim.130
  416.1 3.0 broadcast_in_dim.131
  419.1 1.4 copy.124
  420.5 4.8 %mul.99 = f32[16,2,64,2,128]{4,3,2,0,1:T(2,128)} broadcast(f32[16,2,64,2]{3,2,0,1:T(8,128)} %copy.124), dimensions={0,1,2,3} | broadcast | bytes 2113536 | tf_op jit(solution)/shard_map/mul | solution.py:121
  425.3 3.9 mul.100
  429.2 3.0 fusion.6
  432.2 1.4 reduce_sum.82
  433.6 1.2 div.95
  434.9 0.9 fusion.36
  (44 shorter events, 0.9 us)
Async XLA Ops:
  6.5 2.2 copy-start
  6.5 2.4 copy-start.2
  6.5 2.4 copy-start.8
  6.5 177.3 %reduce-scatter.2.cloned.1.call-start = ((), (), s32[]{:S(2)}) async-start(), calls=%async_computation.3 | async-start | bytes 4456448 | tf_op jit(solution)/shard_map/reduce_scatter | solution.py:71
  14.2 0.7 copy-start.5
  14.2 1.9 copy-start.3
  20.0 165.0 %copy-start.4 = (f32[1024]{0:T(1024)S(1)}, f32[1024]{0:T(1024)}, u32[]{:S(2)}) copy-start(f32[1024]{0:T(1024)} %param.16) | copy-start | bytes 12292
  21.7 165.1 %all-to-all-start = ((bf16[32,2,8256]{2,1,0:T(2,128)(2,1)}), bf16[32,2,8256]{2,1,0:T(2,128)(2,1)}, u32[]{:S(2)}, u32[]{:S(2)}) async-start(bf16[32,2,8256]{2,1,0:T(2,128)(2,1)} %reshape.393), calls=%async_computation.1 | async-start | bytes 2129920 | tf_op jit(solution)/shard_map/all_to_all | solution.py:64
  37.9 233.9 %all-gather.2.cloned.1.call-start = ((), (), s32[]{:S(2)}) async-start(), calls=%async_computation.4 | async-start | bytes 2228224 | tf_op jit(solution)/shard_map/all_gather | solution.py:77
  200.3 71.5 %copy-start.6 = (bf16[1024,256]{1,0:T(8,128)(2,1)S(1)}, bf16[1024,256]{1,0:T(8,128)(2,1)}, u32[]{:S(2)}) copy-start(bf16[1024,256]{1,0:T(8,128)(2,1)} %param.18) | copy-start | bytes 1572868
  274.1 1.0 copy-start.7
  299.1 5.6 %copy-start.9 = (s32[16]{0:T(128)S(1)}, s32[16]{0:T(128)}, u32[]{:S(2)}) copy-start(s32[16]{0:T(128)} %param.21) | copy-start | bytes 196
  299.1 101.8 %all-to-all-start.1 = ((f32[32,1,16640]{2,1,0:T(1,128)}), f32[32,1,16640]{2,1,0:T(1,128)}, u32[]{:S(2)}, u32[]{:S(2)}) async-start(f32[32,1,16640]{2,1,0:T(1,128)} %copy.118), calls=%async_computation.2 | async-start | bytes 4259840 | tf_op jit(solution)/shard_map/all_to_all | solution.py:107
  432.2 3.6 copy-start.1
Sparse Core Ops, SparseCore 0:
  14.3 169.5 reduce-scatter.1
  187.2 84.5 all-gather.1
where the time goes:
time: 444 us; the launch traced here: 443 us
  waiting for transfers between devices  308 us (69%)
  local copies, waits for them, and re-layouts  68 us (15%)
  starting transfers between devices  21.7 us (5%)
  matrix products  15.8 us (4%)
  other arithmetic  15.6 us (4%)
  between operations  13.8 us (3%)
    reduce_scatter x1, waiting for transfers between devices, shards(): lax.psum_scatter(partial_sum, ('tensor', 'enc'), scatter_dimension=0, til...  146 us
    all_to_all x1, waiting for transfers between devices, shards(): lax.all_to_all(reply, 'seq', split_axis=0, concat_axis=0, tiled=True)  96.1 us
    all_gather x1, waiting for transfers between devices, shards(): lax.all_gather(final_piece, ('tensor', 'enc'), axis=0, tiled=True)  65.9 us
    all_to_all x1, starting transfers between devices, shards(): lax.all_to_all(outgoing, 'seq', split_axis=0, concat_axis=0, tiled=True)  16.2 us
    unnamed x24, local copies, waits for them, and re-layouts  9.49 us
  transfers between devices with their start and end apart: 4, of which 3 were waited for; matrix products, arithmetic and copies ran while one was open for 7% of the time, Pallas kernels for 0%

commit v1 on v0

--- a/solution.py
+++ b/solution.py
@@ -74,7 +74,12 @@
     own_rows = lax.dynamic_slice_in_dim(neighbour_rows, piece * piece_rows, piece_rows, axis=0)
     encoded = own_rows.astype(jnp.float32) + reduced
     final_piece = rms_scale(encoded, final_gain).astype(jnp.bfloat16)
-    final_rows = lax.all_gather(final_piece, ("tensor", "enc"), axis=0, tiled=True)
+    final_rows = jnp.concatenate(
+        lax.all_to_all(
+            jnp.stack([final_piece] * lax.axis_size(("tensor", "enc"))), ("tensor", "enc"), 0, 0
+        ),
+        axis=0,
+    )
     key_part = jnp.dot(final_rows, key_weight, preferred_element_type=jnp.float32).astype(
         jnp.bfloat16
     )

time: 444 us -> 474 us (1.068)
  starting transfers between devices: 21.7 us -> 86.3 us
  waiting for transfers between devices: 308 us -> 271 us
    all_gather x1 -> x0, waiting for transfers between devices: 65.9 us -> none  [shards(): lax.all_gather(final_piece, ('tensor', 'enc'), axis=0, tiled=True)]
    all_to_all x1, starting transfers between devices: 5.3 us -> 63.8 us  [shards(): lax.all_to_all(reply, 'seq', split_axis=0, concat_axis=0, tiled=True)]
    all_to_all x0 -> x1, waiting for transfers between devices: none -> 28.9 us  [shards(): lax.all_to_all(jnp.stack([final_piece] * lax.axis_size(('tensor', 'enc'))...]
    all_to_all x0 -> x1, starting transfers between devices: none -> 6.41 us  [shards(): lax.all_to_all(jnp.stack([final_piece] * lax.axis_size(('tensor', 'enc'))...]
    unnamed x24 -> x26, local copies, waits for them, and re-layouts: 9.49 us -> 8.7 us
  transfers between devices with their start and end apart: 4 -> 4, of which waited for: 3 -> 3; matrix products, arithmetic and copies ran while one was open for 7% -> 6% of each run, Pallas kernels for 0% -> 0%
where the time goes in v1:
time: 474 us; the launch traced here: 471 us
  waiting for transfers between devices  271 us (57%)
  starting transfers between devices  86.3 us (18%)
  local copies, waits for them, and re-layouts  68.8 us (15%)
  matrix products  15.9 us (3%)
  other arithmetic  14.9 us (3%)
  between operations  13.8 us (3%)
    reduce_scatter x1, waiting for transfers between devices, shards(): lax.psum_scatter(partial_sum, ('tensor', 'enc'), scatter_dimension=0, til...  146 us
    all_to_all x1, waiting for transfers between devices, shards(): lax.all_to_all(reply, 'seq', split_axis=0, concat_axis=0, tiled=True)  96 us
    all_to_all x1, starting transfers between devices, shards(): lax.all_to_all(reply, 'seq', split_axis=0, concat_axis=0, tiled=True)  63.8 us
    all_to_all x1, waiting for transfers between devices, shards(): lax.all_to_all(jnp.stack([final_piece] * lax.axis_size(('tensor', 'enc'))...  28.9 us
    all_to_all x1, starting transfers between devices, shards(): lax.all_to_all(outgoing, 'seq', split_axis=0, concat_axis=0, tiled=True)  16.1 us
  transfers between devices with their start and end apart: 4, of which 3 were waited for; matrix products, arithmetic and copies ran while one was open for 6% of the time, Pallas kernels for 0%

profile of v1, /device:TPU:1, one launch (start us, length us, event | category | flops | bytes accessed | tf_op | source)
XLA Modules:
  0.0 470.7 jit_solution(362452721265821700)
XLA Ops:
  6.5 2.2 fusion
  8.8 0.1 copy-done.3
  8.9 5.3 %fusion.33 = f32[1024,1024]{1,0:T(8,128)} fusion(bf16[256,1024]{1,0:T(8,128)(2,1)S(1)} %copy-done, bf16[1024,256]{1,0:T(8,128)(2,1)} %param.14, bf16[1024,1024]{1,0:T(8,128)(2,1)S(1)} %copy-done.3, f32[1024]{0:T(1024)S(1)} %copy-done.9, f32[1024]{0:T(1024)S(1)} %add_rsqrt_fusion), kind=kOutput, calls=%fused_computation.42 | convolution fusion | flops 1080295424 | bytes 7348224 | tf_op jit(solution)/shard_map/dot_general | solution.py:70
  14.2 0.7 copy-done.6
  15.0 0.1 reshape.343
  15.1 0.2 convert_reduce_fusion
  15.3 0.1 select_reduce_fusion
  15.4 0.1 fusion.50
  15.5 0.2 reshape.346
  15.8 1.2 gather_fusion
  17.0 0.2 select_select_fusion
  17.2 0.7 gather_fusion.1
  18.1 0.5 broadcast.393
  18.6 1.4 reduce.3
  20.1 1.6 reshape.399
  21.7 16.1 %all-to-all-start.1 = ((bf16[32,2,8256]{2,1,0:T(2,128)(2,1)}), bf16[32,2,8256]{2,1,0:T(2,128)(2,1)S(1)}, u32[]{:S(2)}, u32[]{:S(2)}) async-start(bf16[32,2,8256]{2,1,0:T(2,128)(2,1)} %reshape.399), calls=%async_computation.2 | async-start | bytes 2129920 | tf_op jit(solution)/shard_map/all_to_all | solution.py:64
  37.8 146.1 %reduce-scatter.2.cloned.1.call-done = f32[64,1024]{1,0:T(8,128)} async-done(((f32[1024,1024]{1,0:T(8,128)}), f32[64,1024]{1,0:T(8,128)}) %reduce-scatter.2.cloned.1.call-update) | async-done | bytes 262160 | tf_op jit(solution)/shard_map/reduce_scatter | solution.py:71
  183.9 1.1 multiply_reduce_fusion.1
  185.1 1.1 multiply_convert_fusion
  186.2 1.7 stack.2
  187.8 6.4 %all-to-all-start = ((bf16[16,64,1024]{2,1,0:T(8,128)(2,1)}), bf16[16,64,1024]{2,1,0:T(8,128)(2,1)}, u32[]{:S(2)}, u32[]{:S(2)}) async-start(bf16[16,64,1024]{2,1,0:T(8,128)(2,1)} %stack.2), calls=%async_computation.1 | async-start | bytes 4194304 | tf_op jit(solution)/shard_map/all_to_all | solution.py:78
  194.2 4.4 reshape.400
  198.7 5.3 %copy.112 = bf16[32,1,16512]{0,2,1:T(8,128)(2,1)} copy(bf16[32,1,16512]{2,1,0:T(2,128)(2,1)S(1)} %reshape.400) | data formatting | bytes 2113536 | tf_op jit(solution)/shard_map/all_to_all | solution.py:64
  203.9 3.7 slice.30
  207.6 5.0 %copy.116 = bf16[32,64,2,128]{3,1,2,0:T(8,128)(2,1)} copy(bf16[32,64,2,128]{0,3,2,1:T(8,128)(2,1)} %bitcast.64) | data formatting | bytes 2097152 | tf_op jit(solution)/shard_map/reshape | solution.py:91
  212.6 0.7 compare_and_fusion
  213.3 28.9 %all-to-all-done = bf16[16,64,1024]{2,1,0:T(8,128)(2,1)} async-done(((bf16[16,64,1024]{2,1,0:T(8,128)(2,1)}), bf16[16,64,1024]{2,1,0:T(8,128)(2,1)}, u32[]{:S(2)}, u32[]{:S(2)}) %all-to-all-start) | async-done | bytes 2097184 | tf_op jit(solution)/shard_map/all_to_all | solution.py:78
  242.2 2.4 convolution_convert_fusion
  244.6 2.3 convolution_convert_fusion.1
  246.9 0.1 reshape.345
  247.0 0.1 copy.113
  247.1 0.1 reshape.348
  247.3 0.1 copy.115
  247.4 2.2 gather_fusion.4
  249.6 3.6 multiply_reduce_fusion
  253.2 0.1 reshape_squeeze_broadcast_in_dim.3
  253.3 1.3 fusion.15
  254.6 0.1 reshape.350
  254.7 2.2 gather_fusion.3
  256.9 2.4 fusion.17
  259.2 3.0 copy.117
  262.2 2.9 reshape.349
  265.2 0.1 maximum_bitcast_fusion
  265.3 3.5 copy.118
  268.8 63.8 %all-to-all-start.2 = ((f32[32,1,16640]{2,1,0:T(1,128)}), f32[32,1,16640]{2,1,0:T(1,128)}, u32[]{:S(2)}, u32[]{:S(2)}) async-start(f32[32,1,16640]{2,1,0:T(1,128)} %copy.118), calls=%async_computation.3 | async-start | bytes 4259840 | tf_op jit(solution)/shard_map/all_to_all | solution.py:112
  332.7 0.1 reshape.351
  333.0 96.0 %all-to-all-done.2 = f32[32,1,16640]{2,1,0:T(1,128)} async-done(((f32[32,1,16640]{2,1,0:T(1,128)}), f32[32,1,16640]{2,1,0:T(1,128)}, u32[]{:S(2)}, u32[]{:S(2)}) %all-to-all-start.2) | async-done | bytes 2129952 | tf_op jit(solution)/shard_map/all_to_all | solution.py:112
  429.0 1.7 copy.143
  430.7 2.5 gather_fusion.2
  433.2 3.5 gather.19
  436.7 1.8 copy_select_fusion
  438.9 0.1 reshape.352
  439.0 0.1 broadcast_compare_fusion
  439.1 0.5 copy.123
  439.6 0.2 copy.125
  439.8 4.3 broadcast_in_dim.130
  444.1 3.0 broadcast_in_dim.131
  447.1 1.4 copy.124
  448.5 4.8 %mul.99 = f32[16,2,64,2,128]{4,3,2,0,1:T(2,128)} broadcast(f32[16,2,64,2]{3,2,0,1:T(8,128)} %copy.124), dimensions={0,1,2,3} | broadcast | bytes 2113536 | tf_op jit(solution)/shard_map/mul | solution.py:126
  453.3 3.9 mul.100
  457.2 3.0 fusion.6
  460.2 1.4 reduce_sum.82
  461.7 1.2 div.95
  462.9 0.9 fusion.36
  (46 shorter events, 0.9 us)
Async XLA Ops:
  6.5 2.2 copy-start
  6.5 2.4 copy-start.3
  6.5 2.4 copy-start.9
  6.5 177.4 %reduce-scatter.2.cloned.1.call-start = ((), (), s32[]{:S(2)}) async-start(), calls=%async_computation.4 | async-start | bytes 4456448 | tf_op jit(solution)/shard_map/reduce_scatter | solution.py:71
  14.2 0.7 copy-start.6
  14.2 1.3 copy-start.4
  20.0 165.0 %copy-start.5 = (f32[1024]{0:T(1024)S(1)}, f32[1024]{0:T(1024)}, u32[]{:S(2)}) copy-start(f32[1024]{0:T(1024)} %param.16) | copy-start | bytes 12292
  21.7 164.5 %all-to-all-start.1 = ((bf16[32,2,8256]{2,1,0:T(2,128)(2,1)}), bf16[32,2,8256]{2,1,0:T(2,128)(2,1)S(1)}, u32[]{:S(2)}, u32[]{:S(2)}) async-start(bf16[32,2,8256]{2,1,0:T(2,128)(2,1)} %reshape.399), calls=%async_computation.2 | async-start | bytes 2129920 | tf_op jit(solution)/shard_map/all_to_all | solution.py:64
  186.2 1.7 copy-start.2
  187.8 54.4 %all-to-all-start = ((bf16[16,64,1024]{2,1,0:T(8,128)(2,1)}), bf16[16,64,1024]{2,1,0:T(8,128)(2,1)}, u32[]{:S(2)}, u32[]{:S(2)}) async-start(bf16[16,64,1024]{2,1,0:T(8,128)(2,1)} %stack.2), calls=%async_computation.1 | async-start | bytes 4194304 | tf_op jit(solution)/shard_map/all_to_all | solution.py:78
  207.6 34.6 %copy-start.7 = (bf16[1024,256]{1,0:T(8,128)(2,1)S(1)}, bf16[1024,256]{1,0:T(8,128)(2,1)}, u32[]{:S(2)}) copy-start(bf16[1024,256]{1,0:T(8,128)(2,1)} %param.17) | copy-start | bytes 1572868
  242.2 2.4 copy-start.8
  268.8 64.1 %copy-start.10 = (s32[16]{0:T(128)S(1)}, s32[16]{0:T(128)}, u32[]{:S(2)}) copy-start(s32[16]{0:T(128)} %param.21) | copy-start | bytes 196
  268.8 160.1 %all-to-all-start.2 = ((f32[32,1,16640]{2,1,0:T(1,128)}), f32[32,1,16640]{2,1,0:T(1,128)}, u32[]{:S(2)}, u32[]{:S(2)}) async-start(f32[32,1,16640]{2,1,0:T(1,128)} %copy.118), calls=%async_computation.3 | async-start | bytes 4259840 | tf_op jit(solution)/shard_map/all_to_all | solution.py:112
  460.2 3.6 copy-start.1
Sparse Core Ops, SparseCore 0:
  14.3 169.5 reduce-scatter.1
